TPU v7x, 256 devices: a whole 4x4x8 slice. The times are simulated.
256 devices in a mesh: bus: 16 (over y, z_hi), line: 16 (over z_lo, x, core).
Axes of the slice: x: 4, y: 4, z: 8 (z_hi: 4, z_lo: 2; z = z_hi * 2 + z_lo), core: 2. Of those that a mesh axis runs over, the one named last changes fastest.
Arguments:
- generation: bfloat16 [1024, 16384], P(None, 'bus'), may hold values from -6 to 6
- profiles: float32 [24, 16384], P(None, 'bus'), may hold values from -5 to 5
- scen_profile: int32 [1024], replicated, may hold values from 0 to 23
- ptdf: bfloat16 [16384, 16384], P('line', 'bus'), may hold values from -0.046875 to 0.046875
- lodf: float32 [6144, 512], P('line'), may hold values from -1 to 1
- limits: float32 [6144], P('line'), may hold values from 0.5 to 2
- monitored: int32 [6144], P('line'), may hold values from 0 to 16383, as said below
- outages: int32 [512], replicated, may hold values from 0 to 16383, as said below
- cost_quad: float32 [16384], P('bus'), may hold values from 0.5 to 2
Outputs:
- gradient: bfloat16 [1024, 16384], P('line', 'bus')
- outage_flow: float32 [1024, 512], P('bus')
- outage_sens: float32 [1024, 512], P('bus')
Inputs may be any that keep to these rules, and one draw needn't show every extreme that they name: `monitored`: the entries with positions k * 384 to (k + 1) * 384 - 1 are distinct line ids of the k-th block of 1024 lines (ids k * 1024 to (k + 1) * 1024 - 1). `outages`: distinct line ids; how many fall in each block of 1024 lines varies from block to block.
All inputs are finite; a program needn't handle non-finite values.
Results may differ from a plain program's by a relative error of at most 0.0029.
Values may be sent and summed in bfloat16 or wider, within the bound.
No kernel may reach another device: no remote copies, remote signals or barrier semaphores. Data moves between devices by JAX's collectives and lax.ppermute only.
A program may use at most 64 MiB of HBM per device.

v0:
```python
import math
import jax
import jax.numpy as jnp
from jax import lax
from jax.sharding import PartitionSpec as P

sharpness = 4.0


def contingency(pieces, lodf, limits, outage_total):
    base_block, outage_block = pieces
    post_flow = base_block[:, :, None] + lodf[None, :, :] * outage_block[:, None, :]
    bounds = limits[None, :, None]
    raw_slope = jax.nn.sigmoid(sharpness * (post_flow - bounds)) - jax.nn.sigmoid(
        sharpness * (-post_flow - bounds)
    )
    direct = jnp.sum(raw_slope, axis=2) / outage_total
    sens_part = jnp.einsum("smk,mk->sk", raw_slope, lodf, precision=lax.Precision.HIGHEST)
    return (direct, sens_part)


def on_device(
    generation, profiles, scen_profile, ptdf, lodf, limits, monitored, outages, cost_quad
):
    profile_count = profiles.shape[0]
    profile_pick = (
        scen_profile[:, None] == jnp.arange(profile_count, dtype=jnp.int32)[None, :]
    ).astype(jnp.float32)
    loads = jnp.dot(profile_pick, profiles, precision=lax.Precision.HIGHEST)
    injection = (generation.astype(jnp.float32) - loads).astype(jnp.bfloat16)
    scen_rows = injection.shape[0] // lax.axis_size("bus")
    line_rows = ptdf.shape[0]
    first_line = lax.axis_index("line") * line_rows
    local_monitored = monitored - first_line
    positions = jnp.arange(line_rows, dtype=jnp.int32)
    picker = ((outages - first_line)[None, :] == positions[:, None]).astype(jnp.float32)
    monitor_count = monitored.shape[0]
    inputs = injection
    flow_field = lax.psum_scatter(
        lax.dot_general(inputs, ptdf, (((1,), (1,)), ((), ())), preferred_element_type=jnp.float32),
        "bus",
        scatter_dimension=0,
        tiled=True,
    )
    base = jnp.take(flow_field, local_monitored, axis=1)
    entire_flows = lax.all_gather(flow_field, "line", axis=1, tiled=True)
    outflow = jnp.take(entire_flows, outages, axis=1)
    outage_total = outages.shape[0]
    monitored_total = monitor_count * lax.axis_size("line")
    block_size = math.gcd(scen_rows, 4)
    base_blocks = base.reshape(scen_rows // block_size, block_size, monitor_count)
    outage_blocks = outflow.reshape(scen_rows // block_size, block_size, outage_total)
    direct, sens_part = lax.map(
        lambda pieces: contingency(pieces, lodf, limits, outage_total), (base_blocks, outage_blocks)
    )
    direct = direct.reshape(scen_rows, monitor_count)
    sens_part = sens_part.reshape(scen_rows, outage_total)
    sens_total = lax.psum(sens_part, "line")
    backward = sens_total / outage_total
    outage_sens = sens_total / math.sqrt(monitored_total)
    adjoint = jnp.zeros((scen_rows, line_rows), jnp.float32).at[:, local_monitored].add(direct)
    adjoint = adjoint + jnp.dot(backward, picker.T, precision=lax.Precision.HIGHEST)
    adjoint_half = adjoint.astype(jnp.bfloat16)
    all_adjoint = lax.all_gather(adjoint_half, "bus", axis=0, tiled=True)
    grad_rows = all_adjoint.shape[0] // lax.axis_size("line")
    inputs = all_adjoint
    pushed = lax.psum_scatter(
        jnp.dot(inputs, ptdf, preferred_element_type=jnp.float32),
        "line",
        scatter_dimension=0,
        tiled=True,
    )
    own_generation = lax.dynamic_slice_in_dim(
        generation, lax.axis_index("line") * grad_rows, grad_rows, 0
    ).astype(jnp.float32)
    gradient = (cost_quad[None, :] * own_generation + pushed).astype(jnp.bfloat16)
    return (gradient, outflow, outage_sens)


def solution(mesh):
    placed = (
        P(None, "bus"),
        P(None, "bus"),
        P(),
        P("line", "bus"),
        P("line", None),
        P("line"),
        P("line"),
        P(),
        P("bus"),
    )
    return jax.shard_map(
        on_device,
        mesh=mesh,
        in_specs=placed,
        out_specs=(P("line", "bus"), P("bus", None), P("bus", None)),
        check_vma=False,
    )
```

profile of v0, /device:TPU:24, one launch (start us, length us, event | category | flops | bytes accessed | tf_op | source)
XLA Modules:
  0.0 545.5 jit_solution(11208969200925676231)
XLA Ops:
  7.2 3.7 subtract_convert_fusion
  11.0 4.4 fusion.9
  15.4 98.6 %reduce-scatter.3.cloned.1.call-done = f32[64,1024]{1,0:T(8,128)} async-done(((f32[1024,1024]{1,0:T(8,128)}), f32[64,1024]{1,0:T(8,128)}) %reduce-scatter.3.cloned.1.call-update) | async-done | bytes 262160 | tf_op jit(solution)/shard_map/reduce_scatter | solution.py:39
  116.7 37.6 %all-gather.3.cloned.1.call-done = f32[64,16384]{1,0:T(8,128)} async-done(((f32[64,1024]{1,0:T(8,128)}), f32[64,16384]{1,0:T(8,128)}) %all-gather.3.cloned.1.call-update) | async-done | bytes 4194320 | tf_op jit(solution)/shard_map/all_gather | solution.py:46
  154.3 6.9 %copy.42 = f32[64,16384]{0,1:T(8,128)} copy(f32[64,16384]{1,0:T(8,128)} %all-gather.3.cloned.1.call-done) | data formatting | bytes 8388608 | tf_op jit(solution)/shard_map/all_gather | solution.py:46
  161.2 4.4 gather_fusion.1
  165.8 108.0 %while.12 = (s32[]{:T(128)}, f32[16,4,384]{2,1,0:T(4,128)S(1)}, f32[16,4,512]{2,1,0:T(4,128)S(1)}, f32[16,4,384]{2,1,0:T(4,128)S(1)}, f32[384,512]{1,0:T(8,128)}...) while((s32[]{:T(128)}, f32[16,4,384]{2,1,0:T(4,128)S(1)}, f32[16,4,512]{2,1,0:T(4,128)S(1)}, ...), condition=%wide.region_3.4_spmd, body=%wide.region_1.0_spmd.sunk | while | flops 24377344 | bytes 2462821 | solution.py:53
  169.2 3.3 fusion.17
  176.0 3.3 fusion.17
  182.7 3.3 fusion.17
  189.5 3.3 fusion.17
  196.2 3.3 fusion.17
  202.9 3.3 fusion.17
  206.4 3.3 multiply_reduce_fusion.2
  209.7 3.3 fusion.17
  213.1 3.3 multiply_reduce_fusion.2
  216.4 3.3 fusion.17
  219.9 3.3 multiply_reduce_fusion.2
  223.2 3.3 fusion.17
  226.6 3.3 multiply_reduce_fusion.2
  229.9 3.3 fusion.17
  233.4 3.3 multiply_reduce_fusion.2
  236.7 3.3 fusion.17
  243.4 3.3 fusion.17
  250.2 3.3 fusion.17
  256.9 3.3 fusion.17
  263.7 3.3 fusion.17
  270.4 3.3 fusion.17
  274.8 122.1 %all-reduce.2.cloned.1.call-done = f32[64,512]{1,0:T(8,128)} async-done(((f32[64,512]{1,0:T(8,128)}), f32[64,512]{1,0:T(8,128)}) %all-reduce.2.cloned.1.call-update) | async-done | bytes 131088 | tf_op jit(solution)/shard_map/psum | solution.py:58
  402.5 60.2 %all-gather.5.cloned.1.call-done = bf16[1024,1024]{1,0:T(8,128)(2,1)} async-done(((bf16[64,1024]{1,0:T(8,128)(2,1)}), bf16[1024,1024]{1,0:T(8,128)(2,1)}) %all-gather.5.cloned.1.call-update) | async-done | bytes 2097168 | tf_op jit(solution)/shard_map/all_gather | solution.py:64
  462.7 5.9 %fusion.10 = f32[1024,1024]{1,0:T(8,128)} fusion(bf16[1024,1024]{1,0:T(8,128)(2,1)} %all-gather.5.cloned.1.call-done, bf16[1024,1024]{1,0:T(8,128)(2,1)S(1)} %copy-done), kind=kOutput, calls=%fused_computation.34 | convolution fusion | flops 2147483648 | bytes 8388608 | tf_op jit(solution)/shard_map/dot_general | solution.py:68
  470.2 67.1 %reduce-scatter.5.cloned.1.call-done = f32[64,1024]{1,0:T(8,128)} async-done(((f32[1024,1024]{1,0:T(8,128)}), f32[64,1024]{1,0:T(8,128)}) %reduce-scatter.5.cloned.1.call-update) | async-done | bytes 262160 | tf_op jit(solution)/shard_map/reduce_scatter | solution.py:67
  (122 shorter events, 49.8 us)
Async XLA Ops:
  7.2 3.8 copy-start
  7.2 106.8 %reduce-scatter.3.cloned.1.call-start = ((), (), s32[]{:S(2)}) async-start(), calls=%async_computation.2 | async-start | bytes 4456448 | tf_op jit(solution)/shard_map/reduce_scatter | solution.py:39
  15.3 98.8 %copy-start.4 = (s32[384]{0:T(512)S(1)}, s32[384]{0:T(512)}, u32[]{:S(2)}) copy-start(s32[384]{0:T(512)} %param.17) | copy-start | bytes 4612
  15.3 98.8 %copy-start.2 = (s32[512]{0:T(512)S(1)}, s32[512]{0:T(512)}, u32[]{:S(2)}) copy-start(s32[512]{0:T(512)} %param.18) | copy-start | bytes 6148
  15.4 138.9 %all-gather.3.cloned.1.call-start = ((), (), s32[]{:S(2)}) async-start(), calls=%async_computation.3 | async-start | bytes 4456448 | tf_op jit(solution)/shard_map/all_gather | solution.py:46
  114.0 282.9 %all-reduce.2.cloned.1.call-start = ((), (), s32[]{:S(2)}) async-start(), calls=%async_computation.4 | async-start | bytes 262144 | tf_op jit(solution)/shard_map/psum | solution.py:58
  116.7 49.1 %copy-start.5 = (f32[384]{0:T(512)S(1)}, f32[384]{0:T(512)}, u32[]{:S(2)}) copy-start(f32[384]{0:T(512)} %param.16) | copy-start | bytes 4612
  274.5 188.2 %all-gather.5.cloned.1.call-start = ((), (), s32[]{:S(2)}) async-start(), calls=%async_computation.5 | async-start | bytes 2228224 | tf_op jit(solution)/shard_map/all_gather | solution.py:64
  402.5 134.8 %reduce-scatter.5.cloned.1.call-start = ((), (), s32[]{:S(2)}) async-start(), calls=%async_computation.6 | async-start | bytes 4456448 | tf_op jit(solution)/shard_map/reduce_scatter | solution.py:67
  468.6 1.0 copy-start.1
  468.6 68.7 %copy-start.3 = (f32[1024]{0:T(1024)S(1)}, f32[1024]{0:T(1024)}, u32[]{:S(2)}) copy-start(f32[1024]{0:T(1024)} %param.19) | copy-start | bytes 12292
Sparse Core Ops, SparseCore 0:
  15.5 98.4 reduce-scatter.2
  115.8 38.4 all-gather.2
  274.7 122.1 all-reduce.1
  402.6 60.0 all-gather.4
  468.7 68.4 reduce-scatter.4
where the time goes:
time: 547 us; the launch traced here: 545 us
  waiting for transfers between devices  386 us (71%)
  other arithmetic  112 us (20%)
  local copies, waits for them, and re-layouts  16.8 us (3%)
  matrix products  15.9 us (3%)
  between operations  14 us (3%)
    psum x1, waiting for transfers between devices, on_device(): sens_total = lax.psum(sens_part, 'line')  122 us
    reduce_scatter x1, waiting for transfers between devices, on_device(): lax.psum_scatter(lax.dot_general(inputs, ptdf, (((1,), (1,)), ((), ())),...  98.6 us
    reduce_scatter x1, waiting for transfers between devices, on_device(): lax.psum_scatter(jnp.dot(inputs, ptdf, preferred_element_type=jnp.float32...  67.1 us
    all_gather x1, waiting for transfers between devices, on_device(): all_adjoint = lax.all_gather(adjoint_half, 'bus', axis=0, tiled=True)  60.2 us
    reduce_sum x16, other arithmetic, contingency(): direct = jnp.sum(raw_slope, axis=2) / outage_total  53.5 us
    dot_general x16, other arithmetic, contingency(): jnp.einsum('smk,mk->sk', raw_slope, lodf, precision=lax.Precision.HIGHEST)  53.1 us
    all_gather x1, waiting for transfers between devices, on_device(): entire_flows = lax.all_gather(flow_field, 'line', axis=1, tiled=True)  37.6 us
  transfers between devices with their start and end apart: 5, of which 5 were waited for; matrix products, arithmetic and copies ran while one was open for 1% of the time, Pallas kernels for 0%

commit v1 on v0

--- a/solution.py
+++ b/solution.py
@@ -5,6 +5,11 @@
 from jax.sharding import PartitionSpec as P
 
 sharpness = 4.0
+
+
+def hold_the_block(vector, shard_axis):
+    then = lax.all_gather(vector, axis_name=shard_axis).sum(axis=0)
+    return then
 
 
 def contingency(pieces, lodf, limits, outage_total):
@@ -55,7 +60,7 @@
     )
     direct = direct.reshape(scen_rows, monitor_count)
     sens_part = sens_part.reshape(scen_rows, outage_total)
-    sens_total = lax.psum(sens_part, "line")
+    sens_total = hold_the_block(sens_part, "line")
     backward = sens_total / outage_total
     outage_sens = sens_total / math.sqrt(monitored_total)
     adjoint = jnp.zeros((scen_rows, line_rows), jnp.float32).at[:, local_monitored].add(direct)

time: 547 us -> 460 us (0.84)
  waiting for transfers between devices: 386 us -> 298 us
    psum x1 -> x0, waiting for transfers between devices: 122 us -> none  [on_device(): sens_total = lax.psum(sens_part, 'line')]
    all_gather x0 -> x1, waiting for transfers between devices: none -> 36.4 us  [hold_the_block(): then = lax.all_gather(vector, axis_name=shard_axis).sum(axis=0)]
where the time goes in v1:
time: 460 us; the launch traced here: 459 us
  waiting for transfers between devices  298 us (65%)
  other arithmetic  114 us (25%)
  local copies, waits for them, and re-layouts  16.8 us (4%)
  matrix products  14.9 us (3%)
  between operations  14 us (3%)
    reduce_scatter x1, waiting for transfers between devices, on_device(): lax.psum_scatter(lax.dot_general(inputs, ptdf, (((1,), (1,)), ((), ())),...  98.6 us
    reduce_scatter x1, waiting for transfers between devices, on_device(): lax.psum_scatter(jnp.dot(inputs, ptdf, preferred_element_type=jnp.float32...  67.1 us
    all_gather x1, waiting for transfers between devices, on_device(): all_adjoint = lax.all_gather(adjoint_half, 'bus', axis=0, tiled=True)  58.6 us
    reduce_sum x16, other arithmetic, contingency(): direct = jnp.sum(raw_slope, axis=2) / outage_total  53.5 us
    dot_general x16, other arithmetic, contingency(): jnp.einsum('smk,mk->sk', raw_slope, lodf, precision=lax.Precision.HIGHEST)  53.1 us
    all_gather x1, waiting for transfers between devices, on_device(): entire_flows = lax.all_gather(flow_field, 'line', axis=1, tiled=True)  37.6 us
    all_gather x1, waiting for transfers between devices, hold_the_block(): then = lax.all_gather(vector, axis_name=shard_axis).sum(axis=0)  36.4 us
  transfers between devices with their start and end apart: 5, of which 5 were waited for; matrix products, arithmetic and copies ran while one was open for 1% of the time, Pallas kernels for 0%

profile of v1, /device:TPU:24, one launch (start us, length us, event | category | flops | bytes accessed | tf_op | source)
XLA Modules:
  0.0 459.0 jit_solution(13945753802286077164)
XLA Ops:
  7.2 3.7 subtract_convert_fusion
  11.0 4.4 fusion.9
  15.4 98.6 %reduce-scatter.3.cloned.1.call-done = f32[64,1024]{1,0:T(8,128)} async-done(((f32[1024,1024]{1,0:T(8,128)}), f32[64,1024]{1,0:T(8,128)}) %reduce-scatter.3.cloned.1.call-update) | async-done | bytes 262160 | tf_op jit(solution)/shard_map/reduce_scatter | solution.py:44
  116.7 37.6 %all-gather.4.cloned.1.call-done = f32[64,16384]{1,0:T(8,128)} async-done(((f32[64,1024]{1,0:T(8,128)}), f32[64,16384]{1,0:T(8,128)}) %all-gather.4.cloned.1.call-update) | async-done | bytes 4194320 | tf_op jit(solution)/shard_map/all_gather | solution.py:51
  154.3 6.9 %copy.42 = f32[64,16384]{0,1:T(8,128)} copy(f32[64,16384]{1,0:T(8,128)} %all-gather.4.cloned.1.call-done) | data formatting | bytes 8388608 | tf_op jit(solution)/shard_map/all_gather | solution.py:51
  161.2 4.4 gather_fusion.1
  165.8 108.0 %while.12 = (s32[]{:T(128)}, f32[16,4,384]{2,1,0:T(4,128)S(1)}, f32[16,4,512]{2,1,0:T(4,128)S(1)}, f32[16,4,384]{2,1,0:T(4,128)S(1)}, f32[384,512]{1,0:T(8,128)}...) while((s32[]{:T(128)}, f32[16,4,384]{2,1,0:T(4,128)S(1)}, f32[16,4,512]{2,1,0:T(4,128)S(1)}, ...), condition=%wide.region_3.4_spmd, body=%wide.region_1.0_spmd.sunk | while | flops 24377344 | bytes 2462821 | solution.py:58
  169.2 3.3 fusion.17
  172.6 3.3 multiply_reduce_fusion.2
  175.9 3.3 fusion.17
  179.4 3.3 multiply_reduce_fusion.2
  182.7 3.3 fusion.17
  189.4 3.3 fusion.17
  196.2 3.3 fusion.17
  199.6 3.3 multiply_reduce_fusion.2
  202.9 3.3 fusion.17
  206.4 3.3 multiply_reduce_fusion.2
  209.7 3.3 fusion.17
  216.4 3.3 fusion.17
  223.2 3.3 fusion.17
  226.6 3.3 multiply_reduce_fusion.2
  229.9 3.3 fusion.17
  236.7 3.3 fusion.17
  243.4 3.3 fusion.17
  250.2 3.3 fusion.17
  256.9 3.3 fusion.17
  263.7 3.3 fusion.17
  270.4 3.3 fusion.17
  274.7 36.4 %all-gather.6.cloned.1.call-done = f32[16,64,512]{2,1,0:T(8,128)} async-done(((f32[1,64,512]{2,1,0:T(8,128)}), f32[16,64,512]{2,1,0:T(8,128)}) %all-gather.6.cloned.1.call-update) | async-done | bytes 2097168 | tf_op jit(solution)/shard_map/all_gather | solution.py:11
  317.6 58.6 %all-gather.8.cloned.1.call-done = bf16[1024,1024]{1,0:T(8,128)(2,1)} async-done(((bf16[64,1024]{1,0:T(8,128)(2,1)}), bf16[1024,1024]{1,0:T(8,128)(2,1)}) %all-gather.8.cloned.1.call-update) | async-done | bytes 2097168 | tf_op jit(solution)/shard_map/all_gather | solution.py:69
  376.3 5.9 %fusion.10 = f32[1024,1024]{1,0:T(8,128)} fusion(bf16[1024,1024]{1,0:T(8,128)(2,1)} %all-gather.8.cloned.1.call-done, bf16[1024,1024]{1,0:T(8,128)(2,1)S(1)} %copy-done), kind=kOutput, calls=%fused_computation.34 | convolution fusion | flops 2147483648 | bytes 8388608 | tf_op jit(solution)/shard_map/dot_general | solution.py:73
  383.8 67.1 %reduce-scatter.5.cloned.1.call-done = f32[64,1024]{1,0:T(8,128)} async-done(((f32[1024,1024]{1,0:T(8,128)}), f32[64,1024]{1,0:T(8,128)}) %reduce-scatter.5.cloned.1.call-update) | async-done | bytes 262160 | tf_op jit(solution)/shard_map/reduce_scatter | solution.py:72
  (121 shorter events, 50.7 us)
Async XLA Ops:
  7.2 3.8 copy-start
  7.2 106.8 %reduce-scatter.3.cloned.1.call-start = ((), (), s32[]{:S(2)}) async-start(), calls=%async_computation.2 | async-start | bytes 4456448 | tf_op jit(solution)/shard_map/reduce_scatter | solution.py:44
  15.3 98.8 %copy-start.3 = (s32[384]{0:T(512)S(1)}, s32[384]{0:T(512)}, u32[]{:S(2)}) copy-start(s32[384]{0:T(512)} %param.17) | copy-start | bytes 4612
  15.3 98.8 %copy-start.1 = (s32[512]{0:T(512)S(1)}, s32[512]{0:T(512)}, u32[]{:S(2)}) copy-start(s32[512]{0:T(512)} %param.18) | copy-start | bytes 6148
  15.4 138.9 %all-gather.4.cloned.1.call-start = ((), (), s32[]{:S(2)}) async-start(), calls=%async_computation.3 | async-start | bytes 4456448 | tf_op jit(solution)/shard_map/all_gather | solution.py:51
  114.0 197.1 %all-gather.6.cloned.1.call-start = ((), (), s32[]{:S(2)}) async-start(), calls=%async_computation.4 | async-start | bytes 2228224 | tf_op jit(solution)/shard_map/all_gather | solution.py:11
  116.7 49.2 %copy-start.4 = (f32[384]{0:T(512)S(1)}, f32[384]{0:T(512)}, u32[]{:S(2)}) copy-start(f32[384]{0:T(512)} %param.16) | copy-start | bytes 4612
  274.5 101.8 %all-gather.8.cloned.1.call-start = ((), (), s32[]{:S(2)}) async-start(), calls=%async_computation.5 | async-start | bytes 2228224 | tf_op jit(solution)/shard_map/all_gather | solution.py:69
  317.6 133.2 %reduce-scatter.5.cloned.1.call-start = ((), (), s32[]{:S(2)}) async-start(), calls=%async_computation.6 | async-start | bytes 4456448 | tf_op jit(solution)/shard_map/reduce_scatter | solution.py:72
  382.1 68.7 %copy-start.2 = (f32[1024]{0:T(1024)S(1)}, f32[1024]{0:T(1024)}, u32[]{:S(2)}) copy-start(f32[1024]{0:T(1024)} %param.19) | copy-start | bytes 12292
Sparse Core Ops, SparseCore 0:
  15.5 98.4 reduce-scatter.2
  115.8 38.4 all-gather.3
  274.6 36.4 all-gather.5
  317.7 58.5 all-gather.7
  382.3 68.4 reduce-scatter.4
